TPU v7x, 1024 devices: a whole 4x4x32 slice. The times are simulated.
1024 devices in a mesh: lat: 32 (over y, x, core), lev: 32 (over z).
Axes of the slice: x: 4, y: 4, z: 32, core: 2. Of those that a mesh axis runs over, the one named last changes fastest.
Arguments:
- tracers: float32 [3, 64, 256, 2880], P(None, 'lev', 'lat'), may hold values from -6 to 6
- courant_x: float32 [64, 256, 2880], P('lev', 'lat'), may hold values from -0.8 to 0.8
- courant_y: float32 [64, 256, 2880], P('lev', 'lat'), may hold values from -0.8 to 0.8
- thickness: float32 [256, 2880, 64], P('lat', 'lev'), may hold values from 0.5 to 5
- targets: int32 [256, 2880, 64], P('lat', 'lev'), may hold values from 0 to 31, never falling along the last dimension, each value on 1 to 4 neighbouring positions
Outputs:
- remapped: float32 [3, 32, 256, 2880], P(None, 'lev', 'lat')
Inputs may be any that keep to these rules, and one draw needn't show every extreme that they name: Along the levels of each column the targets never fall; each of the 32 new levels receives 1 to 4 source levels, and in each column one receives exactly 4.
All inputs are finite; a program needn't handle non-finite values.
Results may differ from a plain program's by a relative error of at most 0.0003.
Values sent between devices are 32-bit elements; how exact they have to be, the bound alone decides.
No kernel may reach another device: no remote copies, remote signals or barrier semaphores. Data moves between devices by JAX's collectives and lax.ppermute only.
A program may use at most 64 MiB of HBM per device.

v0:
```python
import jax
import jax.numpy as jnp
from jax import lax
from jax.sharding import PartitionSpec as P

SUBSTEPS = 2


def padded_2(cells, sides, width):
    for axis, dim in sides:
        count = lax.axis_size(axis)
        ends = count - 1
        head = lax.slice_in_dim(cells, 0, width, axis=dim)
        tail = lax.slice_in_dim(cells, cells.shape[dim] - width, cells.shape[dim], axis=dim)
        cells = jnp.concatenate(
            [
                lax.ppermute(tail, axis, [(i, (i + 1) % count) for i in range(ends)]),
                cells,
                lax.ppermute(head, axis, [((i + 1) % count, i) for i in range(ends)]),
            ],
            axis=dim,
        )
    return cells


def ppm_sweep(padded, faces, axis, count):

    def piece(start, stop):
        return lax.slice_in_dim(padded, start, stop, axis=axis)

    face_val = 7.0 / 12.0 * (piece(1, count + 4) + piece(2, count + 5)) - 1.0 / 12.0 * (
        piece(0, count + 3) + piece(3, count + 6)
    )
    cell_midpoint = piece(2, count + 4)
    left_face = lax.slice_in_dim(face_val, 0, count + 2, axis=axis)
    right_face = lax.slice_in_dim(face_val, 1, count + 3, axis=axis)
    slope = right_face - left_face
    curve = 6.0 * (cell_midpoint - 0.5 * (left_face + right_face))

    def lower(x):
        return lax.slice_in_dim(x, 0, count + 1, axis=axis)

    def upper(x):
        return lax.slice_in_dim(x, 1, count + 2, axis=axis)

    from_left = lower(right_face) - 0.5 * faces * (
        lower(slope) - (1.0 - 2.0 * faces / 3.0) * lower(curve)
    )
    from_right = upper(left_face) - 0.5 * faces * (
        upper(slope) + (1.0 + 2.0 * faces / 3.0) * upper(curve)
    )
    flux = faces * jnp.where(faces > 0, from_left, from_right)
    inner = piece(3, count + 3)
    return inner - (
        lax.slice_in_dim(flux, 1, count + 1, axis=axis)
        - lax.slice_in_dim(flux, 0, count, axis=axis)
    )


def lon_sweep(field, courant_x):
    count = field.shape[-1]
    padded = jnp.concatenate([field[..., -3:], field, field[..., :3]], axis=-1)
    faces = jnp.concatenate([courant_x[..., -1:], courant_x], axis=-1)
    return ppm_sweep(padded, faces, 3, count)


def lat_sweep(padded, faces, first_row, total_rows):
    count = padded.shape[2] - 6
    face_rows = first_row - 1 + jnp.arange(count + 1, dtype=jnp.int32)
    valid = ((face_rows >= 0) & (face_rows <= total_rows - 2)).astype(jnp.float32)
    faces = faces * valid[None, :, None]
    swept = ppm_sweep(padded, faces, 2, count)
    cell_rows = first_row + jnp.arange(count, dtype=jnp.int32)
    inside = ((cell_rows >= 0) & (cell_rows < total_rows)).astype(jnp.float32)
    return swept * inside[None, None, :, None]


def local(tracers, courant_x, courant_y, thickness, targets):
    rows = tracers.shape[2]
    kinds = tracers.shape[0]
    total_rows = rows * lax.axis_size("lat")
    first_row = lax.axis_index("lat") * rows
    field = tracers
    for step in range(SUBSTEPS):
        field = lon_sweep(field, courant_x)
        stacked = jnp.concatenate([field, courant_y[None]], axis=0)
        padded = padded_2(stacked, (("lat", 2),), 3)
        field = lat_sweep(padded[:kinds], padded[kinds][:, 2 : rows + 3], first_row, total_rows)
    columns = lax.all_to_all(field, "lev", split_axis=3, concat_axis=1, tiled=True)
    levels_out = columns.shape[1] // 2
    levels = jnp.arange(levels_out, dtype=jnp.int32)

    def remap_row(inputs):
        row_tracers, row_layer_thickness, row_targets = inputs
        indicator_matrix = (row_targets[:, :, None] == levels[None, None, :]).astype(jnp.float32)
        layer_mass = row_tracers * jnp.transpose(row_layer_thickness)[None]
        target_layer_mass = jnp.einsum(
            "mia,gim->gam", indicator_matrix, layer_mass, precision=lax.Precision.HIGHEST
        )
        target_layer_thickness = jnp.einsum(
            "nwi,nw->in", indicator_matrix, row_layer_thickness, precision=lax.Precision.HIGHEST
        )
        return target_layer_mass / target_layer_thickness[None]

    rows_out = lax.map(remap_row, (jnp.transpose(columns, (2, 0, 1, 3)), thickness, targets))
    remapped = jnp.transpose(rows_out, (1, 2, 0, 3))
    return lax.all_to_all(remapped, "lev", split_axis=1, concat_axis=3, tiled=True)


def solution(mesh):
    placed = (
        P(None, "lev", "lat", None),
        P("lev", "lat", None),
        P("lev", "lat", None),
        P("lat", "lev", None),
        P("lat", "lev", None),
    )
    return jax.shard_map(
        local, mesh=mesh, in_specs=placed, out_specs=P(None, "lev", "lat", None), check_vma=False
    )
```

profile of v0, /device:TPU:7, one launch (start us, length us, event | category | flops | bytes accessed | tf_op | source)
XLA Modules:
  0.0 302.5 jit_solution(17460479500107880072)
XLA Ops:
  7.3 1.9 fusion.73
  10.6 3.7 %collective-permute-start = (f32[4,2,3,2880]{3,0,2,1:T(4,128)S(1)}, f32[4,2,3,2880]{3,0,2,1:T(4,128)S(1)}, u32[]{:S(2)}, u32[]{:S(2)}) collective-permute-start(f32[4,2,3,2880]{3,0,2,1:T(4,128)S(1)} %copy.79), channel_id=1, source_target_pairs={{0,32},{32,64},{64,96},{96,128},{128,160},{160,192},{192,224},{224... | collective-permute-start | bytes 829448 | tf_op jit(solution)/shard_map/ppermute | solution.py:17
  14.4 2.1 collective-permute-start.1
  18.0 6.4 %collective-permute-done.1 = f32[4,2,3,2880]{3,0,2,1:T(4,128)S(1)} collective-permute-done((f32[4,2,3,2880]{3,0,2,1:T(4,128)S(1)}, f32[4,2,3,2880]{3,0,2,1:T(4,128)S(1)}, u32[]{:S(2)}, u32[]{:S(2)}) %collective-permute-start.1) | collective-permute-done | bytes 276512 | tf_op jit(solution)/shard_map/ppermute | solution.py:19
  33.8 1.9 fusion.74
  36.7 1.9 collective-permute-start.2
  38.8 2.6 collective-permute-start.3
  42.3 6.4 %collective-permute-done.3 = f32[4,2,3,2880]{3,0,2,1:T(4,128)S(1)} collective-permute-done((f32[4,2,3,2880]{3,0,2,1:T(4,128)S(1)}, f32[4,2,3,2880]{3,0,2,1:T(4,128)S(1)}, u32[]{:S(2)}, u32[]{:S(2)}) %collective-permute-start.3) | collective-permute-done | bytes 276512 | tf_op jit(solution)/shard_map/ppermute | solution.py:19
  53.6 8.3 %copy.92 = f32[3,2,8,2880]{2,0,1,3:T(4,128)} copy(f32[3,2,8,2880]{3,1,2,0:T(2,128)S(1)} %fusion.46) | data formatting | bytes 1105920 | tf_op jit(solution)/shard_map/mul | solution.py:75
  61.9 11.7 %reshape.72 = f32[32,1,4320]{2,1,0:T(1,128)} reshape(f32[2880,2,3,8]{3,2,1,0:T(4,128)} %bitcast.58) | data formatting | bytes 1105920
  73.6 28.5 %all-to-all-start = ((f32[32,1,4320]{2,1,0:T(1,128)}), f32[32,1,4320]{2,1,0:T(1,128)S(1)}, u32[]{:S(2)}, u32[]{:S(2)}) async-start(f32[32,1,4320]{2,1,0:T(1,128)} %reshape.72), calls=%async_computation | async-start | bytes 1114112 | tf_op jit(solution)/shard_map/all_to_all | solution.py:89
  102.1 65.2 %all-to-all-done = f32[32,1,4320]{2,1,0:T(1,128)S(1)} async-done(((f32[32,1,4320]{2,1,0:T(1,128)}), f32[32,1,4320]{2,1,0:T(1,128)S(1)}, u32[]{:S(2)}, u32[]{:S(2)}) %all-to-all-start) | async-done | bytes 552992 | tf_op jit(solution)/shard_map/all_to_all | solution.py:89
  169.7 8.8 %reshape.73 = f32[2880,2,3,8]{3,2,1,0:T(4,128)} reshape(f32[32,4320]{1,0:T(8,128)S(1)} %reduce) | data formatting | bytes 1105920
  178.5 7.7 %copy.104 = f32[3,2,8,32,90]{4,2,1,3,0:T(8,128)S(1)} copy(f32[3,2,8,32,90]{2,0,1,4,3:T(4,128)} %bitcast.59) | data formatting | bytes 1105920 | tf_op jit(solution)/shard_map/all_to_all | solution.py:89
  186.2 58.2 %while.11 = (s32[]{:T(128)}, f32[8,3,32,90]{3,0,1,2:T(8,128)S(1)}, f32[8,3,64,90]{3,0,2,1:T(8,128)S(1)}, f32[8,90,64]{1,2,0:T(8,128)}, s32[8,90,64]{1,2,0:T(8,128)}, /*index=5*/s32[]{:T(128)}, s32[]{:T(128)}) while((s32[]{:T(128)}, f32[8,3,32,90]{3,0,1,2:T(8,128)S(1)}, f32[8,3,64,90]{3,0,2,1:T(8,128)S(1)}, f32[8,90,64]{1,2,0:T(8,128)}, ...), condition=%wide.region_1.2_spmd.clone, body=%wide.region_0.1_spmd.clone.sunk | while | flops 9241922 | bytes 841053 | solution.py:105
  190.8 2.7 dynamic_update_slice.6
  198.1 2.7 dynamic_update_slice.6
  205.4 2.7 dynamic_update_slice.6
  212.6 2.7 dynamic_update_slice.6
  219.9 2.7 dynamic_update_slice.6
  227.2 2.7 dynamic_update_slice.6
  234.5 2.7 dynamic_update_slice.6
  241.7 2.7 dynamic_update_slice.6
  244.4 57.0 %all_to_all.36 = f32[3,32,8,90]{3,2,0,1:T(8,128)S(1)} all-to-all(f32[3,32,8,90]{3,2,0,1:T(8,128)S(1)} %bitcast.67), channel_id=1, replica_groups=mesh['lat'=32,'lev'=32] {'lev'}, dimensions={1} | all-to-all | bytes 552960 | tf_op jit(solution)/shard_map/all_to_all | solution.py:107
  (142 shorter events, 66.1 us)
Async XLA Ops:
  0.0 2.1 copy-start
  9.2 0.9 copy-start.1
  10.6 7.2 %collective-permute-start = (f32[4,2,3,2880]{3,0,2,1:T(4,128)S(1)}, f32[4,2,3,2880]{3,0,2,1:T(4,128)S(1)}, u32[]{:S(2)}, u32[]{:S(2)}) collective-permute-start(f32[4,2,3,2880]{3,0,2,1:T(4,128)S(1)} %copy.79), channel_id=1, source_target_pairs={{0,32},{32,64},{64,96},{96,128},{128,160},{160,192},{192,224},{224... | collective-permute-start | bytes 829448 | tf_op jit(solution)/shard_map/ppermute | solution.py:17
  14.4 10.0 %collective-permute-start.1 = (f32[4,2,3,2880]{3,0,2,1:T(4,128)S(1)}, f32[4,2,3,2880]{3,0,2,1:T(4,128)S(1)}, u32[]{:S(2)}, u32[]{:S(2)}) collective-permute-start(f32[4,2,3,2880]{3,0,2,1:T(4,128)S(1)} %copy.80), channel_id=1, source_target_pairs={{32,0},{64,32},{96,64},{128,96},{160,128},{192,160},{224,192},{256... | collective-permute-start | bytes 829448 | tf_op jit(solution)/shard_map/ppermute | solution.py:19
  36.7 5.4 %collective-permute-start.2 = (f32[4,2,3,2880]{3,0,2,1:T(4,128)S(1)}, f32[4,2,3,2880]{3,0,2,1:T(4,128)S(1)}, u32[]{:S(2)}, u32[]{:S(2)}) collective-permute-start(f32[4,2,3,2880]{3,0,2,1:T(4,128)S(1)} %copy.86), channel_id=1, source_target_pairs={{0,32},{32,64},{64,96},{96,128},{128,160},{160,192},{192,224},{224... | collective-permute-start | bytes 829448 | tf_op jit(solution)/shard_map/ppermute | solution.py:17
  38.8 10.0 %collective-permute-start.3 = (f32[4,2,3,2880]{3,0,2,1:T(4,128)S(1)}, f32[4,2,3,2880]{3,0,2,1:T(4,128)S(1)}, u32[]{:S(2)}, u32[]{:S(2)}) collective-permute-start(f32[4,2,3,2880]{3,0,2,1:T(4,128)S(1)} %copy.87), channel_id=1, source_target_pairs={{32,0},{64,32},{96,64},{128,96},{160,128},{192,160},{224,192},{256... | collective-permute-start | bytes 829448 | tf_op jit(solution)/shard_map/ppermute | solution.py:19
  73.6 93.7 %all-to-all-start = ((f32[32,1,4320]{2,1,0:T(1,128)}), f32[32,1,4320]{2,1,0:T(1,128)S(1)}, u32[]{:S(2)}, u32[]{:S(2)}) async-start(f32[32,1,4320]{2,1,0:T(1,128)} %reshape.72), calls=%async_computation | async-start | bytes 1114112 | tf_op jit(solution)/shard_map/all_to_all | solution.py:89
where the time goes:
time: 304 us; the launch traced here: 302 us
  local copies, waits for them, and re-layouts  81.7 us (27%)
  waiting for transfers between devices  80.1 us (26%)
  blocking collectives  57 us (19%)
  starting transfers between devices  38.8 us (13%)
  other arithmetic  24 us (8%)
  matrix products  20.1 us (7%)
    all_to_all x1, waiting for transfers between devices, local(): lax.all_to_all(field, 'lev', split_axis=3, concat_axis=1, tiled=True)  65.2 us
    all_to_all x1, blocking collectives, local(): lax.all_to_all(remapped, 'lev', split_axis=1, concat_axis=3, tiled=True)  57 us
    all_to_all x1, starting transfers between devices, local(): lax.all_to_all(field, 'lev', split_axis=3, concat_axis=1, tiled=True)  28.5 us
    dynamic_update_slice x16, local copies, waits for them, and re-layouts, local(): lax.map(remap_row, (jnp.transpose(columns, (2, 0, 1, 3)), thickness, targ...  22.2 us
    unnamed x7, local copies, waits for them, and re-layouts  21.1 us
    dynamic_slice x48, local copies, waits for them, and re-layouts, local(): lax.map(remap_row, (jnp.transpose(columns, (2, 0, 1, 3)), thickness, targ...  15.6 us
    ppermute x2, waiting for transfers between devices, padded_2(): lax.ppermute(head, axis, [((i + 1) % count, i) for i in range(ends)])  12.9 us
    dot_general x8, matrix products, remap_row(): jnp.einsum('mia,gim->gam', indicator_matrix, layer_mass, precision=lax.Pr...  10.1 us
  transfers between devices with their start and end apart: 5, of which 5 were waited for; matrix products, arithmetic and copies ran while one was open for 0% of the time, Pallas kernels for 0%

commit v1 on v0

--- a/solution.py
+++ b/solution.py
@@ -75,36 +75,38 @@
     return swept * inside[None, None, :, None]
 
 
+def remap_columns(adv, thick, tg, levels_out):
+    ks = jnp.arange(levels_out, dtype=jnp.int32)
+    member = tg[None] == ks[:, None, None, None]
+    mass = adv * thick[None]
+    new_mass = jnp.sum(jnp.where(member[None], mass[:, None], 0.0), axis=2)
+    new_thick = jnp.sum(jnp.where(member, thick[None], 0.0), axis=1)
+    return jnp.transpose(new_mass / new_thick[None], (1, 0, 2, 3))
+
+
 def local(tracers, courant_x, courant_y, thickness, targets):
     rows = tracers.shape[2]
     kinds = tracers.shape[0]
     total_rows = rows * lax.axis_size("lat")
     first_row = lax.axis_index("lat") * rows
+    parts = lax.axis_size("lev")
+    lon = tracers.shape[3]
+    width = lon // parts
+    levels_out = tracers.shape[1] * parts // 2
     field = tracers
     for step in range(SUBSTEPS):
         field = lon_sweep(field, courant_x)
         stacked = jnp.concatenate([field, courant_y[None]], axis=0)
         padded = padded_2(stacked, (("lat", 2),), 3)
         field = lat_sweep(padded[:kinds], padded[kinds][:, 2 : rows + 3], first_row, total_rows)
-    columns = lax.all_to_all(field, "lev", split_axis=3, concat_axis=1, tiled=True)
-    levels_out = columns.shape[1] // 2
-    levels = jnp.arange(levels_out, dtype=jnp.int32)
-
-    def remap_row(inputs):
-        row_tracers, row_layer_thickness, row_targets = inputs
-        indicator_matrix = (row_targets[:, :, None] == levels[None, None, :]).astype(jnp.float32)
-        layer_mass = row_tracers * jnp.transpose(row_layer_thickness)[None]
-        target_layer_mass = jnp.einsum(
-            "mia,gim->gam", indicator_matrix, layer_mass, precision=lax.Precision.HIGHEST
-        )
-        target_layer_thickness = jnp.einsum(
-            "nwi,nw->in", indicator_matrix, row_layer_thickness, precision=lax.Precision.HIGHEST
-        )
-        return target_layer_mass / target_layer_thickness[None]
-
-    rows_out = lax.map(remap_row, (jnp.transpose(columns, (2, 0, 1, 3)), thickness, targets))
-    remapped = jnp.transpose(rows_out, (1, 2, 0, 3))
-    return lax.all_to_all(remapped, "lev", split_axis=1, concat_axis=3, tiled=True)
+    blocks = jnp.stack([field[..., c * width : (c + 1) * width] for c in range(parts)], axis=0)
+    got = lax.all_to_all(blocks, "lev", split_axis=0, concat_axis=0, tiled=True)
+    adv = jnp.transpose(got, (1, 0, 2, 3, 4)).reshape(kinds, -1, rows, width)
+    thick = jnp.transpose(thickness, (2, 0, 1))
+    tg = jnp.transpose(targets, (2, 0, 1))
+    out = remap_columns(adv, thick, tg, levels_out)
+    back = lax.all_to_all(out, "lev", split_axis=0, concat_axis=0, tiled=True)
+    return jnp.concatenate([back[c] for c in range(parts)], axis=-1)[:, None]
 
 
 def solution(mesh):

time: 304 us -> 236 us (0.78)
  local copies, waits for them, and re-layouts: 81.7 us -> 27 us
  matrix products: 20.1 us -> 0 us
  waiting for transfers between devices: 80.1 us -> 98.8 us
  other arithmetic: 24 us -> 14.1 us
    dynamic_update_slice x16 -> x0, local copies, waits for them, and re-layouts: 22.2 us -> none  [local(): lax.map(remap_row, (jnp.transpose(columns, (2, 0, 1, 3)), thickness, targ...]
    dot_general x16 -> x0, matrix products: 20.1 us -> none  [the longest x8 10.1 us: remap_row(): jnp.einsum('mia,gim->gam', indicator_matrix, layer_mass, precision=lax.Pr...]
    all_to_all x1, waiting for transfers between devices: 65.2 us -> 81.2 us  [local(): got = lax.all_to_all(blocks, 'lev', split_axis=0, concat_axis=0, tiled=True)]
    dynamic_slice x48 -> x0, local copies, waits for them, and re-layouts: 15.6 us -> none  [local(): lax.map(remap_row, (jnp.transpose(columns, (2, 0, 1, 3)), thickness, targ...]
    all_to_all x4 -> x1, local copies, waits for them, and re-layouts: 9.28 us -> 0.06 us  [local(): got = lax.all_to_all(blocks, 'lev', split_axis=0, concat_axis=0, tiled=True)]
    mul x2 -> x0, local copies, waits for them, and re-layouts: 8.37 us -> none  [the longest x1 8.27 us: lat_sweep(): return swept * inside[None, None, :, None]]
    reduce_sum x0 -> x2, other arithmetic: none -> 4.93 us  [the longest x1 3.85 us: remap_columns(): new_mass = jnp.sum(jnp.where(member[None], mass[:, None], 0.0), axis=2)]
    sub x4, other arithmetic: 6.66 us -> 1.99 us  [ppm_sweep(): 7.0 / 12.0 * (piece(1, count + 4) + piece(2, count + 5))]
  transfers between devices with their start and end apart: 5 -> 5, of which waited for: 5 -> 5; matrix products, arithmetic and copies ran while one was open for 0% -> 1% of each run, Pallas kernels for 0% -> 0%
where the time goes in v1:
time: 236 us; the launch traced here: 234 us
  waiting for transfers between devices  98.8 us (42%)
  blocking collectives  55 us (23%)
  starting transfers between devices  38.6 us (16%)
  local copies, waits for them, and re-layouts  27 us (11%)
  other arithmetic  14.1 us (6%)
    all_to_all x1, waiting for transfers between devices, local(): got = lax.all_to_all(blocks, 'lev', split_axis=0, concat_axis=0, tiled=True)  81.2 us
    all_to_all x1, blocking collectives, local(): back = lax.all_to_all(out, 'lev', split_axis=0, concat_axis=0, tiled=True)  55 us
    all_to_all x1, starting transfers between devices, local(): got = lax.all_to_all(blocks, 'lev', split_axis=0, concat_axis=0, tiled=True)  28.6 us
    unnamed x41, local copies, waits for them, and re-layouts  22.2 us
    ppermute x2, waiting for transfers between devices, padded_2(): lax.ppermute(head, axis, [((i + 1) % count, i) for i in range(ends)])  13 us
    ppermute x2, starting transfers between devices, padded_2(): lax.ppermute(tail, axis, [(i, (i + 1) % count) for i in range(ends)])  5.6 us
  transfers between devices with their start and end apart: 5, of which 5 were waited for; matrix products, arithmetic and copies ran while one was open for 1% of the time, Pallas kernels for 0%

profile of v1, /device:TPU:7, one launch (start us, length us, event | category | flops | bytes accessed | tf_op | source)
XLA Modules:
  0.0 233.8 jit_solution(7669353801501191009)
XLA Ops:
  0.0 0.9 fusion.67
  0.9 1.4 concatenate.61
  4.8 0.7 copy-done
  5.6 3.7 %collective-permute-start = (f32[4,2,3,2880]{3,2,1,0:T(4,128)S(1)}, f32[4,2,3,2880]{3,2,1,0:T(4,128)S(1)}, u32[]{:S(2)}, u32[]{:S(2)}) collective-permute-start(f32[4,2,3,2880]{3,2,1,0:T(4,128)S(1)} %get-tuple-element.17), channel_id=1, source_target_pairs={{0,32},{32,64},{64,96},{96,128},{128,160},{160,192},{192,224},{224... | collective-permute-start | bytes 829448 | tf_op jit(solution)/shard_map/ppermute | solution.py:17
  9.3 1.9 collective-permute-start.1
  11.2 2.6 %collective-permute-done = f32[4,2,3,2880]{3,2,1,0:T(4,128)S(1)} collective-permute-done((f32[4,2,3,2880]{3,2,1,0:T(4,128)S(1)}, f32[4,2,3,2880]{3,2,1,0:T(4,128)S(1)}, u32[]{:S(2)}, u32[]{:S(2)}) %collective-permute-start) | collective-permute-done | bytes 276512 | tf_op jit(solution)/shard_map/ppermute | solution.py:17
  13.8 6.5 %collective-permute-done.1 = f32[4,2,3,2880]{3,2,1,0:T(4,128)S(1)} collective-permute-done((f32[4,2,3,2880]{3,2,1,0:T(4,128)S(1)}, f32[4,2,3,2880]{3,2,1,0:T(4,128)S(1)}, u32[]{:S(2)}, u32[]{:S(2)}) %collective-permute-start.1) | collective-permute-done | bytes 276512 | tf_op jit(solution)/shard_map/ppermute | solution.py:19
  24.6 1.9 collective-permute-start.2
  26.6 2.4 %collective-permute-start.3 = (f32[4,2,3,2880]{3,2,1,0:T(4,128)S(1)}, f32[4,2,3,2880]{3,2,1,0:T(4,128)S(1)}, u32[]{:S(2)}, u32[]{:S(2)}) collective-permute-start(f32[4,2,3,2880]{3,2,1,0:T(4,128)S(1)} %get-tuple-element.16), channel_id=1, source_target_pairs={{32,0},{64,32},{96,64},{128,96},{160,128},{192,160},{224,192},{256... | collective-permute-start | bytes 829448 | tf_op jit(solution)/shard_map/ppermute | solution.py:19
  29.0 2.1 collective-permute-done.2
  31.1 6.5 %collective-permute-done.3 = f32[4,2,3,2880]{3,2,1,0:T(4,128)S(1)} collective-permute-done((f32[4,2,3,2880]{3,2,1,0:T(4,128)S(1)}, f32[4,2,3,2880]{3,2,1,0:T(4,128)S(1)}, u32[]{:S(2)}, u32[]{:S(2)}) %collective-permute-start.3) | collective-permute-done | bytes 276512 | tf_op jit(solution)/shard_map/ppermute | solution.py:19
  41.0 0.7 constant_dynamic-update-slice_fusion.29
  45.8 0.7 constant_dynamic-update-slice_fusion.22
  54.6 0.7 constant_dynamic-update-slice_fusion.9
  57.3 0.7 constant_dynamic-update-slice_fusion.5
  59.3 0.7 constant_dynamic-update-slice_fusion.2
  60.0 0.7 constant_dynamic-update-slice_fusion.1
  61.4 28.6 %all-to-all-start = ((f32[32,3,2,8,90]{4,3,2,1,0:T(8,128)}), f32[32,3,2,8,90]{4,3,2,1,0:T(8,128)S(1)}, u32[]{:S(2)}, u32[]{:S(2)}) async-start(f32[32,3,2,8,90]{4,3,2,1,0:T(8,128)} %constant_dynamic-update-slice_fusion), calls=%async_computation | async-start | bytes 1572864 | tf_op jit(solution)/shard_map/all_to_all | solution.py:103
  90.4 1.1 select_reduce_fusion.1
  91.5 1.2 iota_compare_fusion
  92.7 81.2 %all-to-all-done = f32[32,3,2,8,90]{4,3,2,1,0:T(8,128)S(1)} async-done(((f32[32,3,2,8,90]{4,3,2,1,0:T(8,128)}), f32[32,3,2,8,90]{4,3,2,1,0:T(8,128)S(1)}, u32[]{:S(2)}, u32[]{:S(2)}) %all-to-all-start) | async-done | bytes 552992 | tf_op jit(solution)/shard_map/all_to_all | solution.py:103
  174.0 3.9 %select_reduce_fusion = f32[3,32,8,90]{3,2,1,0:T(8,128)S(1)} fusion(f32[3,64,8,90]{3,2,1,0:T(8,128)S(1)} %broadcast_multiply_fusion, pred[32,64,8,90]{3,2,1,0:T(8,128)(4,1)S(1)} %iota_compare_fusion), kind=kLoop, calls=%fused_computation | loop fusion | flops 8778240 | bytes 2304000 | tf_op jit(solution)/shard_map/reduce_sum | solution.py:82
  177.9 55.0 %all_to_all.10 = f32[32,3,8,90]{3,2,1,0:T(8,128)S(1)} all-to-all(f32[32,3,8,90]{3,2,1,0:T(8,128)S(1)} %copy.87), channel_id=1, replica_groups=mesh['lat'=32,'lev'=32] {'lev'}, dimensions={0} | all-to-all | bytes 552960 | tf_op jit(solution)/shard_map/all_to_all | solution.py:108
  232.9 0.9 concatenate.75
  (76 shorter events, 26.9 us)
Async XLA Ops:
  0.0 2.3 copy-start.1
  2.8 0.9 copy-start.4
  4.5 0.9 copy-start
  5.6 8.2 %collective-permute-start = (f32[4,2,3,2880]{3,2,1,0:T(4,128)S(1)}, f32[4,2,3,2880]{3,2,1,0:T(4,128)S(1)}, u32[]{:S(2)}, u32[]{:S(2)}) collective-permute-start(f32[4,2,3,2880]{3,2,1,0:T(4,128)S(1)} %get-tuple-element.17), channel_id=1, source_target_pairs={{0,32},{32,64},{64,96},{96,128},{128,160},{160,192},{192,224},{224... | collective-permute-start | bytes 829448 | tf_op jit(solution)/shard_map/ppermute | solution.py:17
  9.3 11.0 %collective-permute-start.1 = (f32[4,2,3,2880]{3,2,1,0:T(4,128)S(1)}, f32[4,2,3,2880]{3,2,1,0:T(4,128)S(1)}, u32[]{:S(2)}, u32[]{:S(2)}) collective-permute-start(f32[4,2,3,2880]{3,2,1,0:T(4,128)S(1)} %get-tuple-element.18), channel_id=1, source_target_pairs={{32,0},{64,32},{96,64},{128,96},{160,128},{192,160},{224,192},{256... | collective-permute-start | bytes 829448 | tf_op jit(solution)/shard_map/ppermute | solution.py:19
  24.6 6.5 %collective-permute-start.2 = (f32[4,2,3,2880]{3,2,1,0:T(4,128)S(1)}, f32[4,2,3,2880]{3,2,1,0:T(4,128)S(1)}, u32[]{:S(2)}, u32[]{:S(2)}) collective-permute-start(f32[4,2,3,2880]{3,2,1,0:T(4,128)S(1)} %get-tuple-element.15), channel_id=1, source_target_pairs={{0,32},{32,64},{64,96},{96,128},{128,160},{160,192},{192,224},{224... | collective-permute-start | bytes 829448 | tf_op jit(solution)/shard_map/ppermute | solution.py:17
  26.6 11.0 %collective-permute-start.3 = (f32[4,2,3,2880]{3,2,1,0:T(4,128)S(1)}, f32[4,2,3,2880]{3,2,1,0:T(4,128)S(1)}, u32[]{:S(2)}, u32[]{:S(2)}) collective-permute-start(f32[4,2,3,2880]{3,2,1,0:T(4,128)S(1)} %get-tuple-element.16), channel_id=1, source_target_pairs={{32,0},{64,32},{96,64},{128,96},{160,128},{192,160},{224,192},{256... | collective-permute-start | bytes 829448 | tf_op jit(solution)/shard_map/ppermute | solution.py:19
  51.9 38.1 %copy-start.2 = (f32[8,90,64]{1,2,0:T(8,128)S(1)}, f32[8,90,64]{1,2,0:T(8,128)}, u32[]{:S(2)}) copy-start(f32[8,90,64]{1,2,0:T(8,128)} %param.8) | copy-start | bytes 552964
  59.3 30.9 %copy-start.3 = (s32[8,90,64]{1,2,0:T(8,128)S(1)}, s32[8,90,64]{1,2,0:T(8,128)}, u32[]{:S(2)}) copy-start(s32[8,90,64]{1,2,0:T(8,128)} %param.9) | copy-start | bytes 552964
  61.4 112.5 %all-to-all-start = ((f32[32,3,2,8,90]{4,3,2,1,0:T(8,128)}), f32[32,3,2,8,90]{4,3,2,1,0:T(8,128)S(1)}, u32[]{:S(2)}, u32[]{:S(2)}) async-start(f32[32,3,2,8,90]{4,3,2,1,0:T(8,128)} %constant_dynamic-update-slice_fusion), calls=%async_computation | async-start | bytes 1572864 | tf_op jit(solution)/shard_map/all_to_all | solution.py:103
